TPU v7x, 128 devices: a whole 4x4x4 slice. The times are simulated.
128 devices in a mesh: seq: 16 (over z, y), tp: 8 (over x, core).
Axes of the slice: x: 4, y: 4, z: 4, core: 2. Of those that a mesh axis runs over, the one named last changes fastest.
Arguments:
- tokens: bfloat16 [8192, 4096], P(('seq', 'tp')), may hold values from -24 to 24
- w_query: bfloat16 [4096, 4096], P(None, 'tp'), may hold values from -0.09375 to 0.09375
- w_key: bfloat16 [4096, 4096], P(None, 'tp'), may hold values from -0.09375 to 0.09375
- w_value: bfloat16 [4096, 4096], P(None, 'tp'), may hold values from -0.09375 to 0.09375
- w_out: bfloat16 [4096, 4096], P('tp'), may hold values from -0.09375 to 0.09375
- state_in: float32 [32, 128, 128], P('tp'), may hold values from -400 to 400
- grad_out: bfloat16 [8192, 4096], P(('seq', 'tp')), may hold values from -6 to 6
Outputs:
- mixed_out: bfloat16 [8192, 4096], P(('seq', 'tp'))
- input_grad: bfloat16 [8192, 4096], P(('seq', 'tp'))
- query_wgrad: float32 [4096, 4096], P('seq', 'tp')
- key_wgrad: float32 [4096, 4096], P('seq', 'tp')
- value_wgrad: float32 [4096, 4096], P('seq', 'tp')
- out_wgrad: float32 [4096, 4096], P('tp', 'seq')
- state_grad: float32 [32, 128, 128], P('tp', 'seq')
All inputs are finite; a program needn't handle non-finite values.
Results may differ from a plain program's by a relative error of at most 0.02.
Values may be sent and summed in bfloat16 or wider, within the bound.
No kernel may reach another device: no remote copies, remote signals or barrier semaphores. Data moves between devices by JAX's collectives and lax.ppermute only.
A program may use at most 128 MiB of HBM per device.

v0:
```python
import jax
import jax.numpy as jnp
from jax import lax
from jax.sharding import PartitionSpec as P

HIGH = lax.Precision.HIGHEST
ROWS_CONTRACT = (((0,), (0,)), ((), ()))
COLS_CONTRACT = (((1,), (1,)), ((), ()))


def scanned(array, axis):
    count = lax.axis_size(axis)
    place = lax.axis_index(axis)
    total = array
    before = jnp.zeros_like(array)
    after = jnp.zeros_like(array)
    step = 1
    while step < count:
        pairs = [(i, i ^ step) for i in range(count)]
        other = lax.ppermute(total, axis, pairs)
        upper = place & step != 0
        before = before + jnp.where(upper, other, 0.0)
        after = after + jnp.where(upper, 0.0, other)
        total = total + other
        step *= 2
    return (before, after, total)


def body(tokens, w_query, w_key, w_value, w_out, state_in, grad_out):
    head_count = state_in.shape[0]
    head_width = state_in.shape[1]
    rows_all = lax.all_gather(tokens, "tp", axis=0, tiled=True)
    shard_len = rows_all.shape[0]

    def head_split(matrix):
        return matrix.reshape(shard_len, head_count, head_width)

    query = jnp.dot(rows_all, w_query, preferred_element_type=jnp.float32).astype(jnp.bfloat16)
    key_all = jnp.dot(rows_all, w_key, preferred_element_type=jnp.float32).astype(jnp.bfloat16)
    value_all = jnp.dot(rows_all, w_value, preferred_element_type=jnp.float32).astype(jnp.bfloat16)
    query_heads = head_split(query)
    key_heads = head_split(key_all)
    value_heads = head_split(value_all)
    query_full = query_heads.astype(jnp.float32)
    key_full = key_heads.astype(jnp.float32)
    value_full = value_heads.astype(jnp.float32)
    local_kv = jnp.einsum(
        "thd,the->hde", key_heads, value_heads, preferred_element_type=jnp.float32
    )
    earlier, _, _ = scanned(local_kv, "seq")
    state_before = state_in + earlier
    row_ids = lax.broadcasted_iota(jnp.int32, (shard_len, shard_len), 0)
    col_ids = lax.broadcasted_iota(jnp.int32, (shard_len, shard_len), 1)
    mask = (row_ids >= col_ids)[None]
    scores = jnp.einsum("thd,shd->hts", query_heads, key_heads, preferred_element_type=jnp.float32)
    masked = jnp.where(mask, scores, 0.0)
    attn = jnp.einsum("hts,shd->thd", masked, value_full, precision=HIGH) + jnp.einsum(
        "thd,hde->the", query_full, state_before, precision=HIGH
    )
    inverse = lax.rsqrt(jnp.mean(attn * attn, axis=-1, keepdims=True) + 1e-05)
    normed = attn * inverse
    heads_out = normed.reshape(shard_len, head_count * head_width).astype(jnp.bfloat16)
    mixed_out = lax.psum_scatter(
        jnp.dot(heads_out, w_out, preferred_element_type=jnp.float32).astype(jnp.bfloat16),
        "tp",
        scatter_dimension=0,
        tiled=True,
    )
    grad_all = lax.all_gather(grad_out, "tp", axis=0, tiled=True)
    out_part = lax.dot_general(
        heads_out, grad_all, ROWS_CONTRACT, preferred_element_type=jnp.float32
    )
    d_normed = lax.dot_general(grad_all, w_out, COLS_CONTRACT, preferred_element_type=jnp.float32)
    d_normed = d_normed.reshape(shard_len, head_count, head_width)
    d_attn = inverse * (d_normed - normed * jnp.mean(d_normed * normed, axis=-1, keepdims=True))
    local_adj = jnp.einsum("thd,the->hde", query_full, d_attn, precision=HIGH)
    _, later, adj_total = scanned(local_adj, "seq")
    rows_per = head_width // lax.axis_size("seq")
    state_grad = lax.dynamic_slice_in_dim(
        adj_total, lax.axis_index("seq") * rows_per, rows_per, axis=1
    )
    mixed_s = jnp.where(mask, jnp.einsum("the,she->hts", d_attn, value_full, precision=HIGH), 0.0)
    grad_q = jnp.einsum("the,hde->thd", d_attn, state_before, precision=HIGH) + jnp.einsum(
        "hts,shd->thd", mixed_s, key_full, precision=HIGH
    )
    grad_k = jnp.einsum("hts,thd->shd", mixed_s, query_full, precision=HIGH) + jnp.einsum(
        "hde,she->shd", later, value_full, precision=HIGH
    )
    grad_v = jnp.einsum("hts,the->she", masked, d_attn, precision=HIGH) + jnp.einsum(
        "hde,shd->she", later, key_full, precision=HIGH
    )
    query_grad = grad_q.reshape(shard_len, head_count * head_width).astype(jnp.bfloat16)
    key_grad = grad_k.reshape(shard_len, head_count * head_width).astype(jnp.bfloat16)
    value_grad = grad_v.reshape(shard_len, head_count * head_width).astype(jnp.bfloat16)
    term = lax.dot_general(query_grad, w_query, COLS_CONTRACT, preferred_element_type=jnp.float32)
    term = term + lax.dot_general(
        key_grad, w_key, COLS_CONTRACT, preferred_element_type=jnp.float32
    )
    input_grad = lax.psum_scatter(
        (
            term
            + lax.dot_general(
                value_grad, w_value, COLS_CONTRACT, preferred_element_type=jnp.float32
            )
        ).astype(jnp.bfloat16),
        "tp",
        scatter_dimension=0,
        tiled=True,
    )
    query_part = lax.dot_general(
        rows_all, query_grad, ROWS_CONTRACT, preferred_element_type=jnp.float32
    )
    key_part = lax.dot_general(
        rows_all, key_grad, ROWS_CONTRACT, preferred_element_type=jnp.float32
    )
    value_part = lax.dot_general(
        rows_all, value_grad, ROWS_CONTRACT, preferred_element_type=jnp.float32
    )
    query_sum, key_sum, value_sum, out_summed = (
        lax.psum_scatter(
            query_part.astype(jnp.bfloat16), "seq", scatter_dimension=0, tiled=True
        ).astype(jnp.float32),
        lax.psum_scatter(
            key_part.astype(jnp.bfloat16), "seq", scatter_dimension=0, tiled=True
        ).astype(jnp.float32),
        lax.psum_scatter(
            value_part.astype(jnp.bfloat16), "seq", scatter_dimension=0, tiled=True
        ).astype(jnp.float32),
        lax.psum_scatter(
            out_part.astype(jnp.bfloat16), "seq", scatter_dimension=1, tiled=True
        ).astype(jnp.float32),
    )
    grad_scale = lax.rsqrt(jnp.float32(shard_len * lax.axis_size("seq")))
    return (
        mixed_out,
        input_grad,
        query_sum * grad_scale,
        key_sum * grad_scale,
        value_sum * grad_scale,
        out_summed * grad_scale,
        state_grad,
    )


def solution(mesh):
    return jax.shard_map(
        body,
        mesh=mesh,
        in_specs=(
            P(("seq", "tp"), None),
            P(None, "tp"),
            P(None, "tp"),
            P(None, "tp"),
            P("tp", None),
            P("tp", None, None),
            P(("seq", "tp"), None),
        ),
        out_specs=(
            P(("seq", "tp"), None),
            P(("seq", "tp"), None),
            P("seq", "tp"),
            P("seq", "tp"),
            P("seq", "tp"),
            P("tp", "seq"),
            P("tp", "seq", None),
        ),
        check_vma=False,
    )
```

profile of v0, /device:TPU:0, one launch (start us, length us, event | category | flops | bytes accessed | tf_op | source)
XLA Modules:
  0.0 514.8 jit_solution(3716976327167864774)
XLA Ops:
  8.7 35.6 %all-gather.3.cloned.1.call-done = bf16[512,4096]{1,0:T(8,128)(2,1)} async-done(((bf16[64,4096]{1,0:T(8,128)(2,1)}), bf16[512,4096]{1,0:T(8,128)(2,1)}) %all-gather.3.cloned.1.call-update) | async-done | bytes 4194320 | tf_op jit(solution)/shard_map/all_gather | solution.py:32
  44.3 6.0 %convolution_convert_fusion.5 = bf16[512,512]{0,1:T(8,128)(2,1)S(1)} fusion(bf16[512,4096]{1,0:T(8,128)(2,1)} %all-gather.3.cloned.1.call-done, bf16[4096,512]{1,0:T(8,128)(2,1)} %param.9), kind=kOutput, calls=%fused_computation.34 | convolution fusion | flops 2147745792 | bytes 8912896 | tf_op jit(solution)/shard_map/dot_general | solution.py:39
  50.3 2.4 convolution_convert_fusion.7
  54.6 6.9 %collective-permute-done = f32[4,128,128]{2,1,0:T(8,128)S(1)} collective-permute-done((f32[4,128,128]{2,1,0:T(8,128)S(1)}, f32[4,128,128]{2,1,0:T(8,128)S(1)}, u32[]{:S(2)}, u32[]{:S(2)}) %collective-permute-start) | collective-permute-done | bytes 262176 | tf_op jit(solution)/shard_map/ppermute | solution.py:20
  61.6 3.1 collective-permute-start.1
  64.6 6.0 %convolution_convert_fusion.6 = bf16[512,512]{0,1:T(8,128)(2,1)S(1)} fusion(bf16[512,4096]{1,0:T(8,128)(2,1)} %all-gather.3.cloned.1.call-done, bf16[4096,512]{1,0:T(8,128)(2,1)} %param.8), kind=kOutput, calls=%fused_computation.35 | convolution fusion | flops 2147745792 | bytes 8912896 | tf_op jit(solution)/shard_map/dot_general | solution.py:38
  73.3 4.9 collective-permute-done.2
  78.3 3.4 collective-permute-start.3
  81.7 2.8 fusion.9
  84.5 2.0 collective-permute-done.3
  87.4 5.9 %multiply_reduce_fusion = (f32[512,4]{0,1:T(4,128)S(1)}, f32[512,512]{0,1:T(8,128)S(1)}) fusion(f32[512,4,128]{0,2,1:T(8,128)S(1)} %get-tuple-element.17, f32[512,4]{0,1:T(4,128)S(1)} %add_rsqrt_fusion, bf16[512,4096]{1,0:T(8,128)(2,1)} %all-gather.5.cloned.1.call-done, bf16[512,4096]{1,0:T(8,128)(2,1)} %param.11), kind=kOutput, calls=%fused_computation.41 | convolution fusion | flops 2148268032 | bytes 10502144 | tf_op jit(solution)/shard_map/dot_general | solution.py:73
  96.3 2.8 fusion.5
  100.9 4.6 fusion
  106.5 6.5 %convolution_convert_fusion = bf16[512,4096]{1,0:T(8,128)(2,1)} fusion(bf16[512,512]{0,1:T(8,128)(2,1)S(1)} %bitcast.92, bf16[512,4096]{1,0:T(8,128)(2,1)} %all-gather.5.cloned.1.call-done), kind=kOutput, calls=%fused_computation.1 | convolution fusion | flops 2149580800 | bytes 8912896 | tf_op jit(solution)/shard_map/dot_general | solution.py:70
  114.9 7.0 %collective-permute-done.4 = f32[4,128,128]{2,1,0:T(8,128)S(1)} collective-permute-done((f32[4,128,128]{2,1,0:T(8,128)S(1)}, f32[4,128,128]{2,1,0:T(8,128)S(1)}, u32[]{:S(2)}, u32[]{:S(2)}) %collective-permute-start.4) | collective-permute-done | bytes 262176 | tf_op jit(solution)/shard_map/ppermute | solution.py:20
  123.3 8.7 %collective-permute-done.5 = f32[4,128,128]{2,1,0:T(8,128)S(1)} collective-permute-done((f32[4,128,128]{2,1,0:T(8,128)S(1)}, f32[4,128,128]{2,1,0:T(8,128)S(1)}, u32[]{:S(2)}, u32[]{:S(2)}) %collective-permute-start.5) | collective-permute-done | bytes 262176 | tf_op jit(solution)/shard_map/ppermute | solution.py:20
  132.0 2.2 collective-permute-start.6
  134.2 7.7 %collective-permute-done.6 = f32[4,128,128]{2,1,0:T(8,128)S(1)} collective-permute-done((f32[4,128,128]{2,1,0:T(8,128)S(1)}, f32[4,128,128]{2,1,0:T(8,128)S(1)}, u32[]{:S(2)}, u32[]{:S(2)}) %collective-permute-start.6) | collective-permute-done | bytes 262176 | tf_op jit(solution)/shard_map/ppermute | solution.py:20
  142.0 5.6 %collective-permute-start.7 = (f32[4,128,128]{2,1,0:T(8,128)S(1)}, f32[4,128,128]{2,1,0:T(8,128)S(1)}, u32[]{:S(2)}, u32[]{:S(2)}) collective-permute-start(f32[4,128,128]{2,1,0:T(8,128)S(1)} %add.106), channel_id=1, source_target_pairs={{0,64},{8,72},{16,80},{24,88},{32,96},{40,104},{48,112},{56,120},{... | collective-permute-start | bytes 786440 | tf_op jit(solution)/shard_map/ppermute | solution.py:20
  147.7 4.2 fusion.19
  154.2 4.3 fusion.1
  159.0 5.2 %fusion.25 = f32[512,4,128]{0,2,1:T(8,128)S(1)} fusion(f32[512,4,128]{0,2,1:T(8,128)S(1)} %get-tuple-element.14, f32[4,512,512]{2,1,0:T(8,128)} %copy-done, pred[512,512]{1,0:T(8,128)(4,1)S(1)} %iota_compare_fusion), kind=kOutput, calls=%fused_computation.32 | convolution fusion | flops 1611661312 | bytes 6553600 | tf_op jit(solution)/shard_map/hts,the->she/dot_general | solution.py:89
  165.6 4.4 fusion.2
  171.0 6.8 %convolution_convert_fusion.4 = bf16[512,4096]{1,0:T(8,128)(2,1)} fusion(bf16[512,512]{0,1:T(8,128)(2,1)S(1)} %bitcast.93, bf16[512,4096]{1,0:T(8,128)(2,1)} %param.11), kind=kOutput, calls=%fused_computation.5 | convolution fusion | flops 2149580800 | bytes 8912896 | tf_op jit(solution)/shard_map/dot_general | solution.py:64
  178.8 4.7 fusion.38
  183.6 5.7 %fusion.40 = f32[512,4096]{1,0:T(8,128)} fusion(bf16[512,512]{0,1:T(8,128)(2,1)S(1)} %bitcast.97, bf16[4096,512]{1,0:T(8,128)(2,1)S(1)} %copy-done.5), kind=kOutput, calls=%fused_computation.63 | convolution fusion | flops 2147483648 | bytes 13107200 | tf_op jit(solution)/shard_map/dot_general | solution.py:96
  189.3 7.8 %add_convert_fusion = bf16[512,4096]{1,0:T(8,128)(2,1)} fusion(f32[512,4096]{1,0:T(8,128)S(1)} %fusion.38, f32[512,4096]{1,0:T(8,128)} %fusion.40, bf16[512,512]{0,1:T(8,128)(2,1)S(1)} %bitcast.99, bf16[4096,512]{1,0:T(8,128)(2,1)S(1)} %copy-done.7), kind=kOutput, calls=%fused_computation | convolution fusion | flops 2153775104 | bytes 25690112 | tf_op jit(solution)/shard_map/dot_general | solution.py:102
  200.4 66.5 %reduce-scatter.17.cloned.1.call-done = bf16[512,256]{1,0:T(8,128)(2,1)} async-done(((bf16[512,4096]{1,0:T(8,128)(2,1)}), bf16[512,256]{1,0:T(8,128)(2,1)}) %reduce-scatter.17.cloned.1.call-update) | async-done | bytes 262160 | tf_op jit(solution)/shard_map/reduce_scatter | solution.py:129
  268.7 78.4 %reduce-scatter.13.cloned.1.call-done = bf16[256,512]{0,1:T(8,128)(2,1)} async-done(((bf16[4096,512]{0,1:T(8,128)(2,1)}), bf16[256,512]{0,1:T(8,128)(2,1)}) %reduce-scatter.13.cloned.1.call-update) | async-done | bytes 262160 | tf_op jit(solution)/shard_map/reduce_scatter | solution.py:123
  349.1 78.6 %reduce-scatter.15.cloned.1.call-done = bf16[256,512]{0,1:T(8,128)(2,1)} async-done(((bf16[4096,512]{0,1:T(8,128)(2,1)}), bf16[256,512]{0,1:T(8,128)(2,1)}) %reduce-scatter.15.cloned.1.call-update) | async-done | bytes 262160 | tf_op jit(solution)/shard_map/reduce_scatter | solution.py:126
  429.7 38.1 %reduce-scatter.7.cloned.1.call-done = bf16[64,4096]{1,0:T(8,128)(2,1)} async-done(((bf16[512,4096]{1,0:T(8,128)(2,1)}), bf16[64,4096]{1,0:T(8,128)(2,1)}) %reduce-scatter.7.cloned.1.call-update) | async-done | bytes 524304 | tf_op jit(solution)/shard_map/reduce_scatter | solution.py:63
  467.9 39.9 %reduce-scatter.9.cloned.1.call-done = bf16[64,4096]{1,0:T(8,128)(2,1)} async-done(((bf16[512,4096]{1,0:T(8,128)(2,1)}), bf16[64,4096]{1,0:T(8,128)(2,1)}) %reduce-scatter.9.cloned.1.call-update) | async-done | bytes 524304 | tf_op jit(solution)/shard_map/reduce_scatter | solution.py:99
  (102 shorter events, 31.6 us)
Async XLA Ops:
  7.2 37.1 %all-gather.3.cloned.1.call-start = ((), (), s32[]{:S(2)}) async-start(), calls=%async_computation.6 | async-start | bytes 4718592 | tf_op jit(solution)/shard_map/all_gather | solution.py:32
  7.9 79.5 %all-gather.5.cloned.1.call-start = ((), (), s32[]{:S(2)}) async-start(), calls=%async_computation.8 | async-start | bytes 4718592 | tf_op jit(solution)/shard_map/all_gather | solution.py:69
  8.6 189.8 %reduce-scatter.11.cloned.1.call-start = ((), (), s32[]{:S(2)}) async-start(), calls=%async_computation.10 | async-start | bytes 4456448 | tf_op jit(solution)/shard_map/reduce_scatter | solution.py:120
  44.3 6.0 %copy-start.6 = (bf16[4096,512]{1,0:T(8,128)(2,1)S(1)}, bf16[4096,512]{1,0:T(8,128)(2,1)}, u32[]{:S(2)}) copy-start(bf16[4096,512]{1,0:T(8,128)(2,1)} %param.10) | copy-start | bytes 12582916
  44.3 6.0 %copy-start.21 = (bf16[512,4096]{1,0:T(8,128)(2,1)S(1)}, bf16[512,4096]{1,0:T(8,128)(2,1)}, u32[]{:S(2)}) copy-start(bf16[512,4096]{1,0:T(8,128)(2,1)} %all-gather.3.cloned.1.call-done) | copy-start | bytes 12582916
  52.7 29.0 %copy-start.2 = (bf16[512,512]{0,1:T(8,128)(2,1)}, bf16[512,512]{0,1:T(8,128)(2,1)S(1)}, u32[]{:S(2)}) copy-start(bf16[512,512]{0,1:T(8,128)(2,1)S(1)} %convolution_convert_fusion.7) | copy-start | bytes 1572868
  53.0 8.5 %collective-permute-start = (f32[4,128,128]{2,1,0:T(8,128)S(1)}, f32[4,128,128]{2,1,0:T(8,128)S(1)}, u32[]{:S(2)}, u32[]{:S(2)}) collective-permute-start(f32[4,128,128]{2,1,0:T(8,128)S(1)} %fusion.36), channel_id=1, source_target_pairs={{0,8},{8,0},{16,24},{24,16},{32,40},{40,32},{48,56},{56,48},{64,72... | collective-permute-start | bytes 786440 | tf_op jit(solution)/shard_map/ppermute | solution.py:20
  61.6 9.3 %collective-permute-start.1 = (f32[4,128,128]{2,1,0:T(8,128)S(1)}, f32[4,128,128]{2,1,0:T(8,128)S(1)}, u32[]{:S(2)}, u32[]{:S(2)}) collective-permute-start(f32[4,128,128]{2,1,0:T(8,128)S(1)} %add.90), channel_id=1, source_target_pairs={{0,16},{8,24},{16,0},{24,8},{32,48},{40,56},{48,32},{56,40},{64,80... | collective-permute-start | bytes 786440 | tf_op jit(solution)/shard_map/ppermute | solution.py:20
  70.9 7.3 %collective-permute-start.2 = (f32[4,128,128]{2,1,0:T(8,128)S(1)}, f32[4,128,128]{2,1,0:T(8,128)S(1)}, u32[]{:S(2)}, u32[]{:S(2)}) collective-permute-start(f32[4,128,128]{2,1,0:T(8,128)S(1)} %add.92), channel_id=1, source_target_pairs={{0,32},{8,40},{16,48},{24,56},{32,0},{40,8},{48,16},{56,24},{64,96... | collective-permute-start | bytes 786440 | tf_op jit(solution)/shard_map/ppermute | solution.py:20
  73.3 13.3 %copy-start = (f32[4,512,512]{2,1,0:T(8,128)}, f32[4,512,512]{2,1,0:T(8,128)S(1)}, u32[]{:S(2)}) copy-start(f32[4,512,512]{2,1,0:T(8,128)S(1)} %fusion.35) | copy-start | bytes 12582916
  73.3 13.2 %copy-start.20 = (f32[4,128,128]{2,1,0:T(8,128)S(1)}, f32[4,128,128]{2,1,0:T(8,128)}, u32[]{:S(2)}) copy-start(f32[4,128,128]{2,1,0:T(8,128)} %param.12) | copy-start | bytes 786436
  78.3 8.2 %collective-permute-start.3 = (f32[4,128,128]{2,1,0:T(8,128)S(1)}, f32[4,128,128]{2,1,0:T(8,128)S(1)}, u32[]{:S(2)}, u32[]{:S(2)}) collective-permute-start(f32[4,128,128]{2,1,0:T(8,128)S(1)} %add.94), channel_id=1, source_target_pairs={{0,64},{8,72},{16,80},{24,88},{32,96},{40,104},{48,112},{56,120},{... | collective-permute-start | bytes 786440 | tf_op jit(solution)/shard_map/ppermute | solution.py:20
  87.4 7.0 %copy-start.3 = (bf16[512,512]{0,1:T(8,128)(2,1)S(1)}, bf16[512,512]{0,1:T(8,128)(2,1)}, u32[]{:S(2)}) copy-start(bf16[512,512]{0,1:T(8,128)(2,1)} %copy-done.2) | copy-start | bytes 1572868
  96.3 4.6 copy-start.22
  105.5 161.4 %reduce-scatter.17.cloned.1.call-start = ((), (), s32[]{:S(2)}) async-start(), calls=%async_computation.13 | async-start | bytes 4456448 | tf_op jit(solution)/shard_map/reduce_scatter | solution.py:129
  113.0 234.2 %reduce-scatter.13.cloned.1.call-start = ((), (), s32[]{:S(2)}) async-start(), calls=%async_computation.11 | async-start | bytes 4456448 | tf_op jit(solution)/shard_map/reduce_scatter | solution.py:123
  113.7 8.2 %collective-permute-start.4 = (f32[4,128,128]{2,1,0:T(8,128)S(1)}, f32[4,128,128]{2,1,0:T(8,128)S(1)}, u32[]{:S(2)}, u32[]{:S(2)}) collective-permute-start(f32[4,128,128]{2,1,0:T(8,128)S(1)} %fusion.39), channel_id=1, source_target_pairs={{0,8},{8,0},{16,24},{24,16},{32,40},{40,32},{48,56},{56,48},{64,72... | collective-permute-start | bytes 786440 | tf_op jit(solution)/shard_map/ppermute | solution.py:20
  121.9 10.1 %collective-permute-start.5 = (f32[4,128,128]{2,1,0:T(8,128)S(1)}, f32[4,128,128]{2,1,0:T(8,128)S(1)}, u32[]{:S(2)}, u32[]{:S(2)}) collective-permute-start(f32[4,128,128]{2,1,0:T(8,128)S(1)} %add.102), channel_id=1, source_target_pairs={{0,16},{8,24},{16,0},{24,8},{32,48},{40,56},{48,32},{56,40},{64,80... | collective-permute-start | bytes 786440 | tf_op jit(solution)/shard_map/ppermute | solution.py:20
  132.0 21.5 %copy-start.4 = (bf16[512,512]{0,1:T(8,128)(2,1)S(1)}, bf16[512,512]{0,1:T(8,128)(2,1)}, u32[]{:S(2)}) copy-start(bf16[512,512]{0,1:T(8,128)(2,1)} %copy-done.2) | copy-start | bytes 1572868
  132.0 9.9 %collective-permute-start.6 = (f32[4,128,128]{2,1,0:T(8,128)S(1)}, f32[4,128,128]{2,1,0:T(8,128)S(1)}, u32[]{:S(2)}, u32[]{:S(2)}) collective-permute-start(f32[4,128,128]{2,1,0:T(8,128)S(1)} %add.104), channel_id=1, source_target_pairs={{0,32},{8,40},{16,48},{24,56},{32,0},{40,8},{48,16},{56,24},{64,96... | collective-permute-start | bytes 786440 | tf_op jit(solution)/shard_map/ppermute | solution.py:20
  142.0 12.1 %copy-start.18 = (f32[4,128,128]{2,1,0:T(8,128)}, f32[4,128,128]{2,1,0:T(8,128)S(1)}, u32[]{:S(2)}) copy-start(f32[4,128,128]{2,1,0:T(8,128)S(1)} %add.106) | copy-start | bytes 786436
  142.0 12.2 %copy-start.23 = (bf16[512,4096]{1,0:T(8,128)(2,1)S(1)}, bf16[512,4096]{1,0:T(8,128)(2,1)}, u32[]{:S(2)}) copy-start(bf16[512,4096]{1,0:T(8,128)(2,1)} %all-gather.3.cloned.1.call-done) | copy-start | bytes 12582916
  142.0 11.4 %collective-permute-start.7 = (f32[4,128,128]{2,1,0:T(8,128)S(1)}, f32[4,128,128]{2,1,0:T(8,128)S(1)}, u32[]{:S(2)}, u32[]{:S(2)}) collective-permute-start(f32[4,128,128]{2,1,0:T(8,128)S(1)} %add.106), channel_id=1, source_target_pairs={{0,64},{8,72},{16,80},{24,88},{32,96},{40,104},{48,112},{56,120},{... | collective-permute-start | bytes 786440 | tf_op jit(solution)/shard_map/ppermute | solution.py:20
  154.2 4.3 copy-start.14
  158.5 269.2 %reduce-scatter.15.cloned.1.call-start = ((), (), s32[]{:S(2)}) async-start(), calls=%async_computation.12 | async-start | bytes 4456448 | tf_op jit(solution)/shard_map/reduce_scatter | solution.py:126
  159.0 6.6 %copy-start.24 = (bf16[512,4096]{1,0:T(8,128)(2,1)S(1)}, bf16[512,4096]{1,0:T(8,128)(2,1)}, u32[]{:S(2)}) copy-start(bf16[512,4096]{1,0:T(8,128)(2,1)} %all-gather.3.cloned.1.call-done) | copy-start | bytes 12582916
  170.0 297.9 %reduce-scatter.7.cloned.1.call-start = ((), (), s32[]{:S(2)}) async-start(), calls=%async_computation.7 | async-start | bytes 4718592 | tf_op jit(solution)/shard_map/reduce_scatter | solution.py:63
  177.8 5.8 %copy-start.15 = (bf16[512,4,128]{0,2,1:T(8,128)(2,1)S(1)}, bf16[512,4,128]{0,2,1:T(8,128)(2,1)}, u32[]{:S(2)}) copy-start(bf16[512,4,128]{0,2,1:T(8,128)(2,1)} %copy-done.14) | copy-start | bytes 1572868
  177.8 329.9 %reduce-scatter.9.cloned.1.call-start = ((), (), s32[]{:S(2)}) async-start(), calls=%async_computation.9 | async-start | bytes 4718592 | tf_op jit(solution)/shard_map/reduce_scatter | solution.py:99
  178.8 4.8 copy-start.5
  183.6 5.7 %copy-start.7 = (bf16[4096,512]{1,0:T(8,128)(2,1)S(1)}, bf16[4096,512]{1,0:T(8,128)(2,1)}, u32[]{:S(2)}) copy-start(bf16[4096,512]{1,0:T(8,128)(2,1)} %param.10) | copy-start | bytes 12582916
  183.6 5.7 %copy-start.17 = (bf16[512,4,128]{0,2,1:T(8,128)(2,1)S(1)}, bf16[512,4,128]{0,2,1:T(8,128)(2,1)}, u32[]{:S(2)}) copy-start(bf16[512,4,128]{0,2,1:T(8,128)(2,1)} %copy-done.16) | copy-start | bytes 1572868
  (9 other events, 12.8 us)
Sparse Core Ops, SparseCore 0:
  9.7 34.5 all-gather.2
  46.0 32.0 all-gather.4
  105.6 80.6 reduce-scatter.10
  189.9 77.0 reduce-scatter.16
  270.1 77.0 reduce-scatter.12
  350.7 76.9 reduce-scatter.14
  430.7 37.1 reduce-scatter.6
  470.8 36.8 reduce-scatter.8
where the time goes:
time: 522 us; the launch traced here: 515 us
  waiting for transfers between devices  378 us (72%)
  matrix products  86.3 us (17%)
  starting transfers between devices  21 us (4%)
  between operations  14.8 us (3%)
  other arithmetic  7.62 us (1%)
  local copies, waits for them, and re-layouts  7.4 us (1%)
    reduce_scatter x1, waiting for transfers between devices, body(): lax.psum_scatter(value_part.astype(jnp.bfloat16), 'seq', scatter_dimensio...  78.6 us
    reduce_scatter x1, waiting for transfers between devices, body(): lax.psum_scatter(key_part.astype(jnp.bfloat16), 'seq', scatter_dimension=...  78.4 us
    reduce_scatter x1, waiting for transfers between devices, body(): lax.psum_scatter(out_part.astype(jnp.bfloat16), 'seq', scatter_dimension=...  66.5 us
    reduce_scatter x1, waiting for transfers between devices, body(): lax.psum_scatter((term + lax.dot_general(value_grad, w_value, COLS_CONTRA...  39.9 us
    ppermute x8, waiting for transfers between devices, scanned(): other = lax.ppermute(total, axis, pairs)  39.1 us
    reduce_scatter x1, waiting for transfers between devices, body(): lax.psum_scatter(jnp.dot(heads_out, w_out, preferred_element_type=jnp.flo...  38.1 us
    all_gather x1, waiting for transfers between devices, body(): rows_all = lax.all_gather(tokens, 'tp', axis=0, tiled=True)  35.6 us
    ppermute x8, starting transfers between devices, scanned(): other = lax.ppermute(total, axis, pairs)  20.1 us
  transfers between devices with their start and end apart: 16, of which 14 were waited for; matrix products, arithmetic and copies ran while one was open for 15% of the time, Pallas kernels for 0%

commit v1 on v0

--- a/solution.py
+++ b/solution.py
@@ -29,7 +29,11 @@
 def body(tokens, w_query, w_key, w_value, w_out, state_in, grad_out):
     head_count = state_in.shape[0]
     head_width = state_in.shape[1]
-    rows_all = lax.all_gather(tokens, "tp", axis=0, tiled=True)
+    _lead_rings = lambda content: jnp.concatenate(
+        jax.lax.all_to_all(jnp.stack([content] * jax.lax.axis_size("tp"), axis=0), "tp", 0, 0),
+        axis=0,
+    )
+    rows_all = _lead_rings(tokens)
     shard_len = rows_all.shape[0]
 
     def head_split(matrix):

time: 522 us -> 565 us (1.082)
  waiting for transfers between devices: 378 us -> 401 us
  matrix products: 86.3 us -> 95.2 us
  starting transfers between devices: 21 us -> 28 us
    all_to_all x0 -> x1, waiting for transfers between devices: none -> 65.7 us  [body(): jax.lax.all_to_all(jnp.stack([content] * jax.lax.axis_size('tp'), axis=0)...]
    all_gather x1 -> x0, waiting for transfers between devices: 35.6 us -> none  [body(): rows_all = lax.all_gather(tokens, 'tp', axis=0, tiled=True)]
    reduce_scatter x1, waiting for transfers between devices: 66.5 us -> 58.6 us  [body(): lax.psum_scatter(out_part.astype(jnp.bfloat16), 'seq', scatter_dimension=...]
  transfers between devices with their start and end apart: 16 -> 16, of which waited for: 14 -> 13; matrix products, arithmetic and copies ran while one was open for 15% -> 16% of each run, Pallas kernels for 0% -> 0%
where the time goes in v1:
time: 565 us; the launch traced here: 557 us
  waiting for transfers between devices  401 us (71%)
  matrix products  95.2 us (17%)
  starting transfers between devices  28 us (5%)
  between operations  14.7 us (3%)
  local copies, waits for them, and re-layouts  11 us (2%)
  other arithmetic  7.62 us (1%)
    reduce_scatter x1, waiting for transfers between devices, body(): lax.psum_scatter(value_part.astype(jnp.bfloat16), 'seq', scatter_dimensio...  78.6 us
    reduce_scatter x1, waiting for transfers between devices, body(): lax.psum_scatter(key_part.astype(jnp.bfloat16), 'seq', scatter_dimension=...  78.5 us
    all_to_all x1, waiting for transfers between devices, body(): jax.lax.all_to_all(jnp.stack([content] * jax.lax.axis_size('tp'), axis=0)...  65.7 us
    reduce_scatter x1, waiting for transfers between devices, body(): lax.psum_scatter(out_part.astype(jnp.bfloat16), 'seq', scatter_dimension=...  58.6 us
    ppermute x8, waiting for transfers between devices, scanned(): other = lax.ppermute(total, axis, pairs)  40.7 us
    reduce_scatter x1, waiting for transfers between devices, body(): lax.psum_scatter((term + lax.dot_general(value_grad, w_value, COLS_CONTRA...  39.7 us
    reduce_scatter x1, waiting for transfers between devices, body(): lax.psum_scatter(jnp.dot(heads_out, w_out, preferred_element_type=jnp.flo...  38 us
    ppermute x8, starting transfers between devices, scanned(): other = lax.ppermute(total, axis, pairs)  22.6 us
  transfers between devices with their start and end apart: 16, of which 13 were waited for; matrix products, arithmetic and copies ran while one was open for 16% of the time, Pallas kernels for 0%

profile of v1, /device:TPU:0, one launch (start us, length us, event | category | flops | bytes accessed | tf_op | source)
XLA Modules:
  0.0 557.3 jit_solution(8156829097088839962)
XLA Ops:
  7.2 3.6 stack.2
  10.8 4.6 all-to-all-start
  16.1 65.7 %all-to-all-done = bf16[8,64,4096]{2,1,0:T(8,128)(2,1)} async-done(((bf16[8,64,4096]{2,1,0:T(8,128)(2,1)}), bf16[8,64,4096]{2,1,0:T(8,128)(2,1)}, u32[]{:S(2)}, u32[]{:S(2)}) %all-to-all-start) | async-done | bytes 4194336 | tf_op jit(solution)/shard_map/all_to_all | solution.py:33
  81.9 6.0 %convolution_convert_fusion.5 = bf16[512,512]{0,1:T(8,128)(2,1)S(1)} fusion(bf16[512,4096]{1,0:T(8,128)(2,1)} %bitcast, bf16[4096,512]{1,0:T(8,128)(2,1)} %param.9), kind=kOutput, calls=%fused_computation.34 | convolution fusion | flops 2147745792 | bytes 8912896 | tf_op jit(solution)/shard_map/dot_general | solution.py:43
  87.8 4.6 convolution_convert_fusion.7
  94.6 6.1 %collective-permute-done = f32[4,128,128]{2,1,0:T(8,128)S(1)} collective-permute-done((f32[4,128,128]{2,1,0:T(8,128)S(1)}, f32[4,128,128]{2,1,0:T(8,128)S(1)}, u32[]{:S(2)}, u32[]{:S(2)}) %collective-permute-start) | collective-permute-done | bytes 262176 | tf_op jit(solution)/shard_map/ppermute | solution.py:20
  100.7 3.4 collective-permute-start.1
  104.1 5.8 %convolution_convert_fusion.6 = bf16[512,512]{0,1:T(8,128)(2,1)S(1)} fusion(bf16[512,4096]{1,0:T(8,128)(2,1)} %bitcast, bf16[4096,512]{1,0:T(8,128)(2,1)} %param.8), kind=kOutput, calls=%fused_computation.35 | convolution fusion | flops 2147745792 | bytes 8912896 | tf_op jit(solution)/shard_map/dot_general | solution.py:42
  112.7 4.1 collective-permute-done.2
  116.9 4.0 collective-permute-start.3
  126.7 5.9 %multiply_reduce_fusion = (f32[512,4]{0,1:T(4,128)S(1)}, f32[512,512]{0,1:T(8,128)S(1)}) fusion(f32[512,4,128]{0,2,1:T(8,128)S(1)} %get-tuple-element.17, f32[512,4]{0,1:T(4,128)S(1)} %add_rsqrt_fusion, bf16[512,4096]{1,0:T(8,128)(2,1)} %all-gather.2.cloned.1.call-done, bf16[512,4096]{1,0:T(8,128)(2,1)} %param.11), kind=kOutput, calls=%fused_computation.41 | convolution fusion | flops 2148268032 | bytes 10502144 | tf_op jit(solution)/shard_map/dot_general | solution.py:77
  140.2 6.8 %fusion = bf16[4096,512]{0,1:T(8,128)(2,1)} fusion(bf16[512,512]{0,1:T(8,128)(2,1)S(1)} %bitcast.95, bf16[512,4096]{1,0:T(8,128)(2,1)} %bitcast), kind=kOutput, calls=%fused_computation.6 | convolution fusion | flops 2149580800 | bytes 8912896 | tf_op jit(solution)/shard_map/dot_general | solution.py:114
  148.0 6.5 %convolution_convert_fusion = bf16[512,4096]{1,0:T(8,128)(2,1)} fusion(bf16[512,512]{0,1:T(8,128)(2,1)S(1)} %bitcast.93, bf16[512,4096]{1,0:T(8,128)(2,1)} %all-gather.2.cloned.1.call-done), kind=kOutput, calls=%fused_computation.1 | convolution fusion | flops 2149580800 | bytes 8912896 | tf_op jit(solution)/shard_map/dot_general | solution.py:74
  156.0 9.7 %collective-permute-done.4 = f32[4,128,128]{2,1,0:T(8,128)S(1)} collective-permute-done((f32[4,128,128]{2,1,0:T(8,128)S(1)}, f32[4,128,128]{2,1,0:T(8,128)S(1)}, u32[]{:S(2)}, u32[]{:S(2)}) %collective-permute-start.4) | collective-permute-done | bytes 262176 | tf_op jit(solution)/shard_map/ppermute | solution.py:20
  165.7 3.9 collective-permute-start.5
  169.6 6.3 %collective-permute-done.5 = f32[4,128,128]{2,1,0:T(8,128)S(1)} collective-permute-done((f32[4,128,128]{2,1,0:T(8,128)S(1)}, f32[4,128,128]{2,1,0:T(8,128)S(1)}, u32[]{:S(2)}, u32[]{:S(2)}) %collective-permute-start.5) | collective-permute-done | bytes 262176 | tf_op jit(solution)/shard_map/ppermute | solution.py:20
  176.0 3.7 collective-permute-start.6
  179.7 10.0 %collective-permute-done.6 = f32[4,128,128]{2,1,0:T(8,128)S(1)} collective-permute-done((f32[4,128,128]{2,1,0:T(8,128)S(1)}, f32[4,128,128]{2,1,0:T(8,128)S(1)}, u32[]{:S(2)}, u32[]{:S(2)}) %collective-permute-start.6) | collective-permute-done | bytes 262176 | tf_op jit(solution)/shard_map/ppermute | solution.py:20
  189.7 3.2 collective-permute-start.7
  192.9 4.2 fusion.19
  200.2 6.8 %fusion.1 = bf16[4096,512]{0,1:T(8,128)(2,1)} fusion(bf16[512,512]{0,1:T(8,128)(2,1)S(1)} %bitcast.97, bf16[512,4096]{1,0:T(8,128)(2,1)} %bitcast), kind=kOutput, calls=%fused_computation.7 | convolution fusion | flops 2149580800 | bytes 8912896 | tf_op jit(solution)/shard_map/dot_general | solution.py:117
  207.4 5.0 fusion.25
  213.8 6.7 %fusion.2 = bf16[4096,512]{0,1:T(8,128)(2,1)} fusion(bf16[512,512]{0,1:T(8,128)(2,1)S(1)} %bitcast.99, bf16[512,4096]{1,0:T(8,128)(2,1)} %bitcast), kind=kOutput, calls=%fused_computation.8 | convolution fusion | flops 2149580800 | bytes 8912896 | tf_op jit(solution)/shard_map/dot_general | solution.py:120
  221.6 6.6 %convolution_convert_fusion.4 = bf16[512,4096]{1,0:T(8,128)(2,1)} fusion(bf16[512,512]{0,1:T(8,128)(2,1)S(1)} %bitcast.94, bf16[512,4096]{1,0:T(8,128)(2,1)} %param.11), kind=kOutput, calls=%fused_computation.5 | convolution fusion | flops 2149580800 | bytes 8912896 | tf_op jit(solution)/shard_map/dot_general | solution.py:68
  229.3 4.7 fusion.38
  234.0 5.7 %fusion.40 = f32[512,4096]{1,0:T(8,128)} fusion(bf16[512,512]{0,1:T(8,128)(2,1)S(1)} %bitcast.98, bf16[4096,512]{1,0:T(8,128)(2,1)S(1)} %copy-done.5), kind=kOutput, calls=%fused_computation.63 | convolution fusion | flops 2147483648 | bytes 13107200 | tf_op jit(solution)/shard_map/dot_general | solution.py:100
  239.7 8.0 %add_convert_fusion = bf16[512,4096]{1,0:T(8,128)(2,1)} fusion(f32[512,4096]{1,0:T(8,128)S(1)} %fusion.38, f32[512,4096]{1,0:T(8,128)} %fusion.40, bf16[512,512]{0,1:T(8,128)(2,1)S(1)} %bitcast.100, bf16[4096,512]{1,0:T(8,128)(2,1)S(1)} %copy-done.7), kind=kOutput, calls=%fused_computation | convolution fusion | flops 2153775104 | bytes 25690112 | tf_op jit(solution)/shard_map/dot_general | solution.py:106
  251.1 58.6 %reduce-scatter.17.cloned.1.call-done = bf16[512,256]{1,0:T(8,128)(2,1)} async-done(((bf16[512,4096]{1,0:T(8,128)(2,1)}), bf16[512,256]{1,0:T(8,128)(2,1)}) %reduce-scatter.17.cloned.1.call-update) | async-done | bytes 262160 | tf_op jit(solution)/shard_map/reduce_scatter | solution.py:133
  311.5 78.5 %reduce-scatter.13.cloned.1.call-done = bf16[256,512]{0,1:T(8,128)(2,1)} async-done(((bf16[4096,512]{0,1:T(8,128)(2,1)}), bf16[256,512]{0,1:T(8,128)(2,1)}) %reduce-scatter.13.cloned.1.call-update) | async-done | bytes 262160 | tf_op jit(solution)/shard_map/reduce_scatter | solution.py:127
  392.0 78.6 %reduce-scatter.15.cloned.1.call-done = bf16[256,512]{0,1:T(8,128)(2,1)} async-done(((bf16[4096,512]{0,1:T(8,128)(2,1)}), bf16[256,512]{0,1:T(8,128)(2,1)}) %reduce-scatter.15.cloned.1.call-update) | async-done | bytes 262160 | tf_op jit(solution)/shard_map/reduce_scatter | solution.py:130
  472.5 38.0 %reduce-scatter.7.cloned.1.call-done = bf16[64,4096]{1,0:T(8,128)(2,1)} async-done(((bf16[512,4096]{1,0:T(8,128)(2,1)}), bf16[64,4096]{1,0:T(8,128)(2,1)}) %reduce-scatter.7.cloned.1.call-update) | async-done | bytes 524304 | tf_op jit(solution)/shard_map/reduce_scatter | solution.py:67
  510.6 39.7 %reduce-scatter.9.cloned.1.call-done = bf16[64,4096]{1,0:T(8,128)(2,1)} async-done(((bf16[512,4096]{1,0:T(8,128)(2,1)}), bf16[64,4096]{1,0:T(8,128)(2,1)}) %reduce-scatter.9.cloned.1.call-update) | async-done | bytes 524304 | tf_op jit(solution)/shard_map/reduce_scatter | solution.py:103
  (94 shorter events, 37.7 us)
Async XLA Ops:
  10.8 71.1 %all-to-all-start = ((bf16[8,64,4096]{2,1,0:T(8,128)(2,1)}), bf16[8,64,4096]{2,1,0:T(8,128)(2,1)}, u32[]{:S(2)}, u32[]{:S(2)}) async-start(bf16[8,64,4096]{2,1,0:T(8,128)(2,1)} %stack.2), calls=%async_computation | async-start | bytes 8388608 | tf_op jit(solution)/shard_map/all_to_all | solution.py:33
  15.3 111.3 %all-gather.2.cloned.1.call-start = ((), (), s32[]{:S(2)}) async-start(), calls=%async_computation.8 | async-start | bytes 4718592 | tf_op jit(solution)/shard_map/all_gather | solution.py:73
  16.1 233.0 %reduce-scatter.11.cloned.1.call-start = ((), (), s32[]{:S(2)}) async-start(), calls=%async_computation.10 | async-start | bytes 4456448 | tf_op jit(solution)/shard_map/reduce_scatter | solution.py:124
  81.8 6.0 %copy-start.6 = (bf16[4096,512]{1,0:T(8,128)(2,1)S(1)}, bf16[4096,512]{1,0:T(8,128)(2,1)}, u32[]{:S(2)}) copy-start(bf16[4096,512]{1,0:T(8,128)(2,1)} %param.10) | copy-start | bytes 12582916
  92.4 28.4 %copy-start.2 = (bf16[512,512]{0,1:T(8,128)(2,1)}, bf16[512,512]{0,1:T(8,128)(2,1)S(1)}, u32[]{:S(2)}) copy-start(bf16[512,512]{0,1:T(8,128)(2,1)S(1)} %convolution_convert_fusion.7) | copy-start | bytes 1572868
  92.8 7.9 %collective-permute-start = (f32[4,128,128]{2,1,0:T(8,128)S(1)}, f32[4,128,128]{2,1,0:T(8,128)S(1)}, u32[]{:S(2)}, u32[]{:S(2)}) collective-permute-start(f32[4,128,128]{2,1,0:T(8,128)S(1)} %fusion.36), channel_id=1, source_target_pairs={{0,8},{8,0},{16,24},{24,16},{32,40},{40,32},{48,56},{56,48},{64,72... | collective-permute-start | bytes 786440 | tf_op jit(solution)/shard_map/ppermute | solution.py:20
  100.7 9.2 %collective-permute-start.1 = (f32[4,128,128]{2,1,0:T(8,128)S(1)}, f32[4,128,128]{2,1,0:T(8,128)S(1)}, u32[]{:S(2)}, u32[]{:S(2)}) collective-permute-start(f32[4,128,128]{2,1,0:T(8,128)S(1)} %add.90), channel_id=1, source_target_pairs={{0,16},{8,24},{16,0},{24,8},{32,48},{40,56},{48,32},{56,40},{64,80... | collective-permute-start | bytes 786440 | tf_op jit(solution)/shard_map/ppermute | solution.py:20
  110.0 6.9 %collective-permute-start.2 = (f32[4,128,128]{2,1,0:T(8,128)S(1)}, f32[4,128,128]{2,1,0:T(8,128)S(1)}, u32[]{:S(2)}, u32[]{:S(2)}) collective-permute-start(f32[4,128,128]{2,1,0:T(8,128)S(1)} %add.92), channel_id=1, source_target_pairs={{0,32},{8,40},{16,48},{24,56},{32,0},{40,8},{48,16},{56,24},{64,96... | collective-permute-start | bytes 786440 | tf_op jit(solution)/shard_map/ppermute | solution.py:20
  112.7 13.2 %copy-start = (f32[4,512,512]{2,1,0:T(8,128)}, f32[4,512,512]{2,1,0:T(8,128)S(1)}, u32[]{:S(2)}) copy-start(f32[4,512,512]{2,1,0:T(8,128)S(1)} %fusion.35) | copy-start | bytes 12582916
  112.7 13.1 %copy-start.20 = (f32[4,128,128]{2,1,0:T(8,128)S(1)}, f32[4,128,128]{2,1,0:T(8,128)}, u32[]{:S(2)}) copy-start(f32[4,128,128]{2,1,0:T(8,128)} %param.12) | copy-start | bytes 786436
  116.9 8.9 %collective-permute-start.3 = (f32[4,128,128]{2,1,0:T(8,128)S(1)}, f32[4,128,128]{2,1,0:T(8,128)S(1)}, u32[]{:S(2)}, u32[]{:S(2)}) collective-permute-start(f32[4,128,128]{2,1,0:T(8,128)S(1)} %add.94), channel_id=1, source_target_pairs={{0,64},{8,72},{16,80},{24,88},{32,96},{40,104},{48,112},{56,120},{... | collective-permute-start | bytes 786440 | tf_op jit(solution)/shard_map/ppermute | solution.py:20
  126.7 7.0 %copy-start.3 = (bf16[512,512]{0,1:T(8,128)(2,1)S(1)}, bf16[512,512]{0,1:T(8,128)(2,1)}, u32[]{:S(2)}) copy-start(bf16[512,512]{0,1:T(8,128)(2,1)} %copy-done.2) | copy-start | bytes 1572868
  135.6 3.8 copy-start.1
  135.6 2.8 copy-start.9
  147.0 162.7 %reduce-scatter.17.cloned.1.call-start = ((), (), s32[]{:S(2)}) async-start(), calls=%async_computation.13 | async-start | bytes 4456448 | tf_op jit(solution)/shard_map/reduce_scatter | solution.py:133
  154.5 235.5 %reduce-scatter.13.cloned.1.call-start = ((), (), s32[]{:S(2)}) async-start(), calls=%async_computation.11 | async-start | bytes 4456448 | tf_op jit(solution)/shard_map/reduce_scatter | solution.py:127
  155.2 10.5 %collective-permute-start.4 = (f32[4,128,128]{2,1,0:T(8,128)S(1)}, f32[4,128,128]{2,1,0:T(8,128)S(1)}, u32[]{:S(2)}, u32[]{:S(2)}) collective-permute-start(f32[4,128,128]{2,1,0:T(8,128)S(1)} %fusion.39), channel_id=1, source_target_pairs={{0,8},{8,0},{16,24},{24,16},{32,40},{40,32},{48,56},{56,48},{64,72... | collective-permute-start | bytes 786440 | tf_op jit(solution)/shard_map/ppermute | solution.py:20
  165.7 10.2 %collective-permute-start.5 = (f32[4,128,128]{2,1,0:T(8,128)S(1)}, f32[4,128,128]{2,1,0:T(8,128)S(1)}, u32[]{:S(2)}, u32[]{:S(2)}) collective-permute-start(f32[4,128,128]{2,1,0:T(8,128)S(1)} %add.102), channel_id=1, source_target_pairs={{0,16},{8,24},{16,0},{24,8},{32,48},{40,56},{48,32},{56,40},{64,80... | collective-permute-start | bytes 786440 | tf_op jit(solution)/shard_map/ppermute | solution.py:20
  176.0 23.6 %copy-start.4 = (bf16[512,512]{0,1:T(8,128)(2,1)S(1)}, bf16[512,512]{0,1:T(8,128)(2,1)}, u32[]{:S(2)}) copy-start(bf16[512,512]{0,1:T(8,128)(2,1)} %copy-done.2) | copy-start | bytes 1572868
  176.0 13.7 %collective-permute-start.6 = (f32[4,128,128]{2,1,0:T(8,128)S(1)}, f32[4,128,128]{2,1,0:T(8,128)S(1)}, u32[]{:S(2)}, u32[]{:S(2)}) collective-permute-start(f32[4,128,128]{2,1,0:T(8,128)S(1)} %add.104), channel_id=1, source_target_pairs={{0,32},{8,40},{16,48},{24,56},{32,0},{40,8},{48,16},{56,24},{64,96... | collective-permute-start | bytes 786440 | tf_op jit(solution)/shard_map/ppermute | solution.py:20
  189.7 10.4 %copy-start.18 = (f32[4,128,128]{2,1,0:T(8,128)}, f32[4,128,128]{2,1,0:T(8,128)S(1)}, u32[]{:S(2)}) copy-start(f32[4,128,128]{2,1,0:T(8,128)S(1)} %add.106) | copy-start | bytes 786436
  189.7 9.7 %collective-permute-start.7 = (f32[4,128,128]{2,1,0:T(8,128)S(1)}, f32[4,128,128]{2,1,0:T(8,128)S(1)}, u32[]{:S(2)}, u32[]{:S(2)}) collective-permute-start(f32[4,128,128]{2,1,0:T(8,128)S(1)} %add.106), channel_id=1, source_target_pairs={{0,64},{8,72},{16,80},{24,88},{32,96},{40,104},{48,112},{56,120},{... | collective-permute-start | bytes 786440 | tf_op jit(solution)/shard_map/ppermute | solution.py:20
  200.2 6.8 %copy-start.14 = (bf16[512,4,128]{0,2,1:T(8,128)(2,1)}, bf16[512,4,128]{0,2,1:T(8,128)(2,1)S(1)}, u32[]{:S(2)}) copy-start(bf16[512,4,128]{0,2,1:T(8,128)(2,1)S(1)} %fusion.29) | copy-start | bytes 1572868
  207.0 263.6 %reduce-scatter.15.cloned.1.call-start = ((), (), s32[]{:S(2)}) async-start(), calls=%async_computation.12 | async-start | bytes 4456448 | tf_op jit(solution)/shard_map/reduce_scatter | solution.py:130
  220.6 1.1 copy-start.11
  220.6 290.0 %reduce-scatter.7.cloned.1.call-start = ((), (), s32[]{:S(2)}) async-start(), calls=%async_computation.7 | async-start | bytes 4718592 | tf_op jit(solution)/shard_map/reduce_scatter | solution.py:67
  228.2 1.1 copy-start.13
  228.2 5.8 %copy-start.15 = (bf16[512,4,128]{0,2,1:T(8,128)(2,1)S(1)}, bf16[512,4,128]{0,2,1:T(8,128)(2,1)}, u32[]{:S(2)}) copy-start(bf16[512,4,128]{0,2,1:T(8,128)(2,1)} %copy-done.14) | copy-start | bytes 1572868
  228.2 322.1 %reduce-scatter.9.cloned.1.call-start = ((), (), s32[]{:S(2)}) async-start(), calls=%async_computation.9 | async-start | bytes 4718592 | tf_op jit(solution)/shard_map/reduce_scatter | solution.py:103
  229.2 4.8 copy-start.5
  234.0 5.7 %copy-start.7 = (bf16[4096,512]{1,0:T(8,128)(2,1)S(1)}, bf16[4096,512]{1,0:T(8,128)(2,1)}, u32[]{:S(2)}) copy-start(bf16[4096,512]{1,0:T(8,128)(2,1)} %param.10) | copy-start | bytes 12582916
  234.0 5.7 %copy-start.17 = (bf16[512,4,128]{0,2,1:T(8,128)(2,1)S(1)}, bf16[512,4,128]{0,2,1:T(8,128)(2,1)}, u32[]{:S(2)}) copy-start(bf16[512,4,128]{0,2,1:T(8,128)(2,1)} %copy-done.16) | copy-start | bytes 1572868
  (5 other events, 4.1 us)
Sparse Core Ops, SparseCore 0:
  17.9 53.2 all-gather.1
  147.1 81.8 reduce-scatter.10
  232.7 76.9 reduce-scatter.16
  312.9 77.0 reduce-scatter.12
  393.5 76.9 reduce-scatter.14
  473.4 37.1 reduce-scatter.6
  513.5 36.7 reduce-scatter.8
